TPU v7x, 512 devices: a whole 4x8x8 slice. The times are simulated.
512 devices in a mesh: grp: 16 (over x, z_lo), ep: 32 (over y, z_hi, core).
Axes of the slice: x: 4, y: 8, z: 8 (z_hi: 2, z_lo: 4; z = z_hi * 4 + z_lo), core: 2. Of those that a mesh axis runs over, the one named last changes fastest.
Arguments:
- slot_hidden: bfloat16 [65536, 8, 768], P(('grp', 'ep')), may hold values from -6 to 6
- expert_ids: int32 [65536, 8], P(('grp', 'ep')), may hold values from 0 to 63, all different within a row; in each aligned block of 128 rows (0 to 127, 128 to 255, ...) at most 24 rows name the same one
- gate_fixed: int32 [65536, 8], P(('grp', 'ep')), may hold values from 1 to 65535
- master: float32 [64, 768, 2048], P('ep', 'grp'), may hold values from -6 to 6
- moment_one: bfloat16 [64, 768, 2048], P('ep', 'grp'), may hold values from -3 to 3
- moment_two: bfloat16 [64, 768, 2048], P('ep', 'grp'), may hold values from 0.0099487305 to 2
- gradient: bfloat16 [64, 768, 2048], P('ep', 'grp'), may hold values from -6 to 6
Outputs:
- mixed: bfloat16 [65536, 2048], P(('grp', 'ep'))
- backup: float32 [64, 768, 2048], P('ep', 'grp')
Inputs may be any that keep to these rules, and one draw needn't show every extreme that they name: `expert_ids`: in each aligned block of 128 rows (the rows of one device) no expert is named by more than 24 rows, a bound that some block reaches; the 8 experts of a row differ.
All inputs are finite; a program needn't handle non-finite values.
Results may differ from a plain program's by a relative error of at most 0.0057.
Values may be sent and summed in bfloat16 or wider, within the bound.
No kernel may reach another device: no remote copies, remote signals or barrier semaphores. Data moves between devices by JAX's collectives and lax.ppermute only.
A program may use at most 64 MiB of HBM per device.

v0:
```python
import math
import jax
import jax.numpy as jnp
from jax import lax
from jax.sharding import PartitionSpec as P

beta_one = 0.9
beta_two = 0.95
corr_one = 1.0 - 0.9**40
corr_two = 1.0 - 0.95**40
learn_rate = 0.05
decay_rate = 0.1
adam_eps = 1e-08
gate_unit = 65536.0


def adamw_step(master, moment_one, moment_two, gradient):
    widened = gradient.astype(jnp.float32)
    first_moment = beta_one * moment_one.astype(jnp.float32) + (1.0 - beta_one) * widened
    second_moment = beta_two * moment_two.astype(jnp.float32) + (1.0 - beta_two) * widened * widened
    return (
        first_moment / corr_one / (jnp.sqrt(second_moment / corr_two) + adam_eps)
        + decay_rate * master
    )


def slot_positions(ids, capacity):
    count = ids.shape[0]
    rows = lax.broadcasted_iota(jnp.int32, (count, count), 0)
    cols = lax.broadcasted_iota(jnp.int32, (count, count), 1)
    same = (ids[:, None] == ids[None, :]) & (cols < rows)
    slot_index = jnp.sum(same.astype(jnp.int32), axis=1)
    return ids * capacity + slot_index


def body(slot_hidden, expert_ids, gate_fixed, master, moment_one, moment_two, gradient):
    groups = lax.axis_size("grp")
    ranks = lax.axis_size("ep")
    local_experts = master.shape[0]
    experts = local_experts * ranks
    tok_count, top_count, hidden_width = slot_hidden.shape
    width = master.shape[2]
    capacity = max(2, tok_count * top_count // experts + tok_count * top_count // (2 * experts))
    slots = experts * capacity
    scaling = 1.0 / math.sqrt(hidden_width)
    step_dir = adamw_step(master, moment_one, moment_two, gradient)
    updated = master - learn_rate * step_dir
    weights = updated.astype(jnp.bfloat16)
    gathered = lax.all_gather(weights, "grp", axis=1, tiled=True)
    shift = groups // 2
    backup = lax.ppermute(step_dir, "grp", [(s, (s + shift) % groups) for s in range(groups)])
    pairs = tok_count * top_count
    positions = slot_positions(expert_ids.reshape(pairs), capacity)
    slot_ids = lax.broadcasted_iota(jnp.int32, (slots, pairs), 0)
    placing = (positions[None, :] == slot_ids).astype(jnp.bfloat16)
    outgoing = jnp.dot(
        placing, slot_hidden.reshape(pairs, hidden_width), preferred_element_type=jnp.float32
    ).astype(jnp.bfloat16)
    outgoing = outgoing.reshape(experts, capacity, hidden_width)
    arrived = lax.all_to_all(outgoing, "ep", split_axis=0, concat_axis=1, tiled=True)
    product = jnp.einsum("erh,ehd->erd", arrived, gathered, preferred_element_type=jnp.float32)
    results = (product * scaling).astype(jnp.bfloat16)
    tiles = results.reshape(local_experts, ranks, capacity, width).transpose(1, 0, 2, 3)
    returned = lax.all_to_all(tiles, "ep", split_axis=0, concat_axis=0, tiled=True)
    returned = returned.reshape(slots, width)
    factors = gate_fixed.astype(jnp.float32) / gate_unit
    token_pos = positions.reshape(tok_count, top_count)
    slot_row = lax.broadcasted_iota(jnp.int32, (tok_count, top_count, slots), 2)
    combine = jnp.sum(
        jnp.where(token_pos[:, :, None] == slot_row, factors[:, :, None], 0.0), axis=1
    )
    combine_hi = combine.astype(jnp.bfloat16)
    combine_lo = (combine - combine_hi.astype(jnp.float32)).astype(jnp.bfloat16)
    mixed = jnp.dot(combine_hi, returned, preferred_element_type=jnp.float32) + jnp.dot(
        combine_lo, returned, preferred_element_type=jnp.float32
    )
    return (mixed.astype(jnp.bfloat16), backup)


def solution(mesh):
    tokens = P(("grp", "ep"), None, None)
    pair_spec = P(("grp", "ep"), None)
    state = P("ep", "grp", None)
    in_specs = (tokens, pair_spec, pair_spec, state, state, state, state)
    out_specs = (pair_spec, state)
    return jax.shard_map(body, mesh=mesh, in_specs=in_specs, out_specs=out_specs, check_vma=False)
```

profile of v0, /device:TPU:21, one launch (start us, length us, event | category | flops | bytes accessed | tf_op | source)
XLA Modules:
  0.0 426.3 jit_solution(7426811078113007954)
XLA Ops:
  7.2 0.0 copy-start
  7.2 0.0 all-gather.2.cloned.1.call-start
  7.2 3.3 subtract_convert_fusion.1
  10.5 0.0 all-gather.2.cloned.1.call-update
  10.5 0.8 copy.24
  11.3 0.1 eq.31
  11.4 0.5 convert_reduce_fusion
  11.9 0.0 copy-done
  11.9 3.0 fusion.2
  15.0 75.1 %all_to_all.23 = bf16[64,24,768]{2,1,0:T(8,128)(2,1)S(1)} all-to-all(bf16[64,24,768]{2,1,0:T(8,128)(2,1)S(1)} %bitcast.21), channel_id=1, replica_groups=mesh['grp'=16,'ep'=32] {'ep'}, dimensions={0} | all-to-all | bytes 4718592 | tf_op jit(solution)/shard_map/all_to_all | solution.py:60
  90.1 1.6 copy.28
  91.6 118.8 %all-gather.2.cloned.1.call-done = bf16[2,768,2048]{2,1,0:T(8,128)(2,1)} async-done(((bf16[2,48,2048]{2,1,0:T(8,128)(2,1)}), bf16[2,768,2048]{2,1,0:T(8,128)(2,1)}) %all-gather.2.cloned.1.call-update) | async-done | bytes 6291472 | tf_op jit(solution)/shard_map/all_gather | solution.py:49
  210.5 7.9 %multiply_convert_fusion = bf16[2,768,2048]{2,1,0:T(8,128)(2,1)S(1)} fusion(bf16[2,768,768]{2,1,0:T(8,128)(2,1)} %bitcast.20, bf16[2,768,2048]{2,1,0:T(8,128)(2,1)} %all-gather.2.cloned.1.call-done), kind=kOutput, calls=%fused_computation | convolution fusion | flops 4838129664 | bytes 14942208 | tf_op jit(solution)/shard_map/erh,ehd->erd/dot_general | solution.py:61
  218.3 3.2 copy.31
  221.6 0.0 copy-start.1
  221.6 0.0 copy-start.2
  221.6 11.1 %all-to-all-start.1 = ((bf16[32,2,24,2048]{3,2,1,0:T(8,128)(2,1)}), bf16[32,2,24,2048]{3,2,1,0:T(8,128)(2,1)}, u32[]{:S(2)}, u32[]{:S(2)}) async-start(bf16[32,2,24,2048]{3,2,1,0:T(8,128)(2,1)} %bitcast.17), calls=%async_computation.1 | async-start | bytes 12582912 | tf_op jit(solution)/shard_map/all_to_all | solution.py:64
  232.7 4.1 collective-permute-start
  236.7 0.1 reduce_sum.21
  236.9 0.0 copy-done.1
  236.9 0.1 copy.26
  237.0 0.0 copy-done.2
  237.0 0.1 copy.27
  237.1 2.0 select_reduce_fusion
  239.2 16.0 %collective-permute-done = f32[2,48,2048]{2,1,0:T(8,128)S(1)} collective-permute-done((f32[2,48,2048]{2,1,0:T(8,128)}, f32[2,48,2048]{2,1,0:T(8,128)S(1)}, u32[]{:S(2)}, u32[]{:S(2)}) %collective-permute-start) | collective-permute-done | bytes 786464 | tf_op jit(solution)/shard_map/ppermute | solution.py:51
  255.1 155.0 %all-to-all-done.1 = bf16[32,2,24,2048]{3,2,1,0:T(8,128)(2,1)} async-done(((bf16[32,2,24,2048]{3,2,1,0:T(8,128)(2,1)}), bf16[32,2,24,2048]{3,2,1,0:T(8,128)(2,1)}, u32[]{:S(2)}, u32[]{:S(2)}) %all-to-all-start.1) | async-done | bytes 6291488 | tf_op jit(solution)/shard_map/all_to_all | solution.py:64
  410.1 3.8 fusion.15
  413.9 4.7 %fusion.4 = bf16[128,2048]{1,0:T(8,128)(2,1)} fusion(f32[128,2048]{1,0:T(8,128)S(1)} %fusion.15, bf16[1536,2048]{1,0:T(8,128)(2,1)} %bitcast.7, f32[128,1536]{1,0:T(8,128)S(1)} %select_reduce_fusion), kind=kOutput, calls=%fused_computation.12 | convolution fusion | flops 806617088 | bytes 8650752 | tf_op jit(solution)/shard_map/dot_general | solution.py:74
  418.6 0.9 copy.33
  (4 shorter events, 0.1 us)
Async XLA Ops:
  7.2 4.8 %copy-start = (bf16[128,8,768]{2,1,0:T(8,128)(2,1)S(1)}, bf16[128,8,768]{2,1,0:T(8,128)(2,1)}, u32[]{:S(2)}) copy-start(bf16[128,8,768]{2,1,0:T(8,128)(2,1)} %param.7) | copy-start | bytes 4718596
  7.2 203.3 %all-gather.2.cloned.1.call-start = ((), (), s32[]{:S(2)}) async-start(), calls=%async_computation.2 | async-start | bytes 6684672 | tf_op jit(solution)/shard_map/all_gather | solution.py:49
  221.6 15.3 %copy-start.1 = (s32[128,8]{0,1:T(8,128)S(1)}, s32[128,8]{0,1:T(8,128)}, u32[]{:S(2)}) copy-start(s32[128,8]{0,1:T(8,128)} %param.8) | copy-start | bytes 12292
  221.6 15.4 %copy-start.2 = (s32[128,8]{0,1:T(8,128)S(1)}, s32[128,8]{0,1:T(8,128)}, u32[]{:S(2)}) copy-start(s32[128,8]{0,1:T(8,128)} %param.9) | copy-start | bytes 12292
  221.6 188.5 %all-to-all-start.1 = ((bf16[32,2,24,2048]{3,2,1,0:T(8,128)(2,1)}), bf16[32,2,24,2048]{3,2,1,0:T(8,128)(2,1)}, u32[]{:S(2)}, u32[]{:S(2)}) async-start(bf16[32,2,24,2048]{3,2,1,0:T(8,128)(2,1)} %bitcast.17), calls=%async_computation.1 | async-start | bytes 12582912 | tf_op jit(solution)/shard_map/all_to_all | solution.py:64
  232.7 22.5 %collective-permute-start = (f32[2,48,2048]{2,1,0:T(8,128)}, f32[2,48,2048]{2,1,0:T(8,128)S(1)}, u32[]{:S(2)}, u32[]{:S(2)}) collective-permute-start(f32[2,48,2048]{2,1,0:T(8,128)} %get-tuple-element.3), channel_id=1, source_target_pairs={{0,256},{32,288},{64,320},{96,352},{128,384},{160,416},{192,448},{... | collective-permute-start | bytes 2359304 | tf_op jit(solution)/shard_map/ppermute | solution.py:51
Sparse Core Ops, SparseCore 0:
  10.7 199.7 all-gather.1
where the time goes:
time: 427 us; the launch traced here: 426 us
  waiting for transfers between devices  290 us (68%)
  blocking collectives  75.1 us (18%)
  matrix products  19.3 us (5%)
  starting transfers between devices  15.2 us (4%)
  between operations  14.1 us (3%)
  local copies, waits for them, and re-layouts  6.93 us (2%)
  other arithmetic  5.84 us (1%)
    all_to_all x1, waiting for transfers between devices, body(): lax.all_to_all(tiles, 'ep', split_axis=0, concat_axis=0, tiled=True)  155 us
    all_gather x1, waiting for transfers between devices, body(): gathered = lax.all_gather(weights, 'grp', axis=1, tiled=True)  119 us
    all_to_all x1, blocking collectives, body(): lax.all_to_all(outgoing, 'ep', split_axis=0, concat_axis=1, tiled=True)  75.1 us
    ppermute x1, waiting for transfers between devices, body(): lax.ppermute(step_dir, 'grp', [(s, (s + shift) % groups) for s in range(g...  16 us
    all_to_all x1, starting transfers between devices, body(): lax.all_to_all(tiles, 'ep', split_axis=0, concat_axis=0, tiled=True)  11.1 us
  transfers between devices with their start and end apart: 3, of which 3 were waited for; matrix products, arithmetic and copies ran while one was open for 2% of the time, Pallas kernels for 0%

commit v1 on v0

--- a/solution.py
+++ b/solution.py
@@ -57,7 +57,10 @@
         placing, slot_hidden.reshape(pairs, hidden_width), preferred_element_type=jnp.float32
     ).astype(jnp.bfloat16)
     outgoing = outgoing.reshape(experts, capacity, hidden_width)
-    arrived = lax.all_to_all(outgoing, "ep", split_axis=0, concat_axis=1, tiled=True)
+    arrived = jnp.concatenate(
+        lax.all_to_all(jnp.stack(jnp.split(outgoing, lax.axis_size("ep"), axis=0)), "ep", 0, 0),
+        axis=1,
+    )
     product = jnp.einsum("erh,ehd->erd", arrived, gathered, preferred_element_type=jnp.float32)
     results = (product * scaling).astype(jnp.bfloat16)
     tiles = results.reshape(local_experts, ranks, capacity, width).transpose(1, 0, 2, 3)

time: 427 us -> 425 us (level)
  no operation moved by 1% of the time
where the time goes in v1:
time: 425 us
  waiting for transfers between devices  289 us (68%)
  blocking collectives  75.1 us (18%)
  matrix products  19.3 us (5%)
  starting transfers between devices  15.2 us (4%)
  between operations  14.4 us (3%)
  local copies, waits for them, and re-layouts  6.66 us (2%)
  other arithmetic  5.84 us (1%)
    all_to_all x1, waiting for transfers between devices, body(): lax.all_to_all(tiles, 'ep', split_axis=0, concat_axis=0, tiled=True)  154 us
    all_gather x1, waiting for transfers between devices, body(): gathered = lax.all_gather(weights, 'grp', axis=1, tiled=True)  119 us
    all_to_all x1, blocking collectives, body(): lax.all_to_all(jnp.stack(jnp.split(outgoing, lax.axis_size('ep'), axis=0)...  75.1 us
    ppermute x1, waiting for transfers between devices, body(): lax.ppermute(step_dir, 'grp', [(s, (s + shift) % groups) for s in range(g...  16 us
    all_to_all x1, starting transfers between devices, body(): lax.all_to_all(tiles, 'ep', split_axis=0, concat_axis=0, tiled=True)  11.1 us
  transfers between devices with their start and end apart: 3, of which 3 were waited for; matrix products, arithmetic and copies ran while one was open for 2% of the time, Pallas kernels for 0%

profile of v1, /device:TPU:21, one launch (start us, length us, event | category | flops | bytes accessed | tf_op | source)
XLA Modules:
  0.0 425.1 jit_solution(8661065646550280738)
XLA Ops:
  7.2 0.0 copy-start
  7.2 0.0 copy-start.1
  7.2 0.0 all-gather.2.cloned.1.call-start
  7.2 3.3 subtract_convert_fusion.1
  10.5 0.0 all-gather.2.cloned.1.call-update
  10.5 0.0 copy-done.1
  10.5 0.1 copy.24
  10.6 0.1 eq.31
  10.7 0.5 convert_reduce_fusion
  11.3 0.0 copy-done
  11.3 3.0 fusion.2
  14.3 0.1 fusion.19
  14.6 0.1 fusion.18
  15.0 75.1 %all_to_all.10 = bf16[32,2,24,768]{3,2,1,0:T(8,128)(2,1)S(1)} all-to-all(bf16[32,2,24,768]{3,2,1,0:T(8,128)(2,1)S(1)} %constant_dynamic-update-slice_fusion), channel_id=1, replica_groups=mesh['grp'=16,'ep'=32] {'ep'}, dimensions={0} | all-to-all | bytes 4718592 | tf_op jit(solution)/shard_map/all_to_all | solution.py:61
  90.1 1.6 copy.28
  91.7 118.8 %all-gather.2.cloned.1.call-done = bf16[2,768,2048]{2,1,0:T(8,128)(2,1)} async-done(((bf16[2,48,2048]{2,1,0:T(8,128)(2,1)}), bf16[2,768,2048]{2,1,0:T(8,128)(2,1)}) %all-gather.2.cloned.1.call-update) | async-done | bytes 6291472 | tf_op jit(solution)/shard_map/all_gather | solution.py:49
  210.5 7.8 %multiply_convert_fusion = bf16[2,768,2048]{2,1,0:T(8,128)(2,1)S(1)} fusion(bf16[2,768,768]{2,1,0:T(8,128)(2,1)} %bitcast.49, bf16[2,768,2048]{2,1,0:T(8,128)(2,1)} %all-gather.2.cloned.1.call-done), kind=kOutput, calls=%fused_computation | convolution fusion | flops 4838129664 | bytes 14942208 | tf_op jit(solution)/shard_map/erh,ehd->erd/dot_general | solution.py:64
  218.4 3.2 copy.31
  221.6 0.0 copy-start.2
  221.6 11.1 %all-to-all-start.1 = ((bf16[32,2,24,2048]{3,2,1,0:T(8,128)(2,1)}), bf16[32,2,24,2048]{3,2,1,0:T(8,128)(2,1)}, u32[]{:S(2)}, u32[]{:S(2)}) async-start(bf16[32,2,24,2048]{3,2,1,0:T(8,128)(2,1)} %bitcast.46), calls=%async_computation.1 | async-start | bytes 12582912 | tf_op jit(solution)/shard_map/all_to_all | solution.py:67
  232.7 4.1 collective-permute-start
  236.7 0.1 reduce_sum.21
  236.9 0.1 copy.26
  237.0 0.0 copy-done.2
  237.0 0.1 copy.27
  237.1 2.0 select_reduce_fusion
  239.2 16.0 %collective-permute-done = f32[2,48,2048]{2,1,0:T(8,128)S(1)} collective-permute-done((f32[2,48,2048]{2,1,0:T(8,128)}, f32[2,48,2048]{2,1,0:T(8,128)S(1)}, u32[]{:S(2)}, u32[]{:S(2)}) %collective-permute-start) | collective-permute-done | bytes 786464 | tf_op jit(solution)/shard_map/ppermute | solution.py:51
  255.1 153.8 %all-to-all-done.1 = bf16[32,2,24,2048]{3,2,1,0:T(8,128)(2,1)} async-done(((bf16[32,2,24,2048]{3,2,1,0:T(8,128)(2,1)}), bf16[32,2,24,2048]{3,2,1,0:T(8,128)(2,1)}, u32[]{:S(2)}, u32[]{:S(2)}) %all-to-all-start.1) | async-done | bytes 6291488 | tf_op jit(solution)/shard_map/all_to_all | solution.py:67
  408.9 3.8 fusion.15
  412.7 4.7 %fusion.4 = bf16[128,2048]{1,0:T(8,128)(2,1)} fusion(f32[128,2048]{1,0:T(8,128)S(1)} %fusion.15, bf16[1536,2048]{1,0:T(8,128)(2,1)} %bitcast.37, f32[128,1536]{1,0:T(8,128)S(1)} %select_reduce_fusion), kind=kOutput, calls=%fused_computation.12 | convolution fusion | flops 806617088 | bytes 8650752 | tf_op jit(solution)/shard_map/dot_general | solution.py:77
  417.4 0.9 copy.64
  (36 shorter events, 0.3 us)
Async XLA Ops:
  7.2 4.1 copy-start
  7.2 3.3 copy-start.1
  7.2 203.3 %all-gather.2.cloned.1.call-start = ((), (), s32[]{:S(2)}) async-start(), calls=%async_computation.2 | async-start | bytes 6684672 | tf_op jit(solution)/shard_map/all_gather | solution.py:49
  221.6 15.4 %copy-start.2 = (s32[128,8]{0,1:T(8,128)S(1)}, s32[128,8]{0,1:T(8,128)}, u32[]{:S(2)}) copy-start(s32[128,8]{0,1:T(8,128)} %param.9) | copy-start | bytes 12292
  221.6 187.3 %all-to-all-start.1 = ((bf16[32,2,24,2048]{3,2,1,0:T(8,128)(2,1)}), bf16[32,2,24,2048]{3,2,1,0:T(8,128)(2,1)}, u32[]{:S(2)}, u32[]{:S(2)}) async-start(bf16[32,2,24,2048]{3,2,1,0:T(8,128)(2,1)} %bitcast.46), calls=%async_computation.1 | async-start | bytes 12582912 | tf_op jit(solution)/shard_map/all_to_all | solution.py:67
  232.7 22.5 %collective-permute-start = (f32[2,48,2048]{2,1,0:T(8,128)}, f32[2,48,2048]{2,1,0:T(8,128)S(1)}, u32[]{:S(2)}, u32[]{:S(2)}) collective-permute-start(f32[2,48,2048]{2,1,0:T(8,128)} %get-tuple-element.3), channel_id=1, source_target_pairs={{0,256},{32,288},{64,320},{96,352},{128,384},{160,416},{192,448},{... | collective-permute-start | bytes 2359304 | tf_op jit(solution)/shard_map/ppermute | solution.py:51
Sparse Core Ops, SparseCore 0:
  10.7 199.7 all-gather.1

commit v2 on v0

--- a/solution.py
+++ b/solution.py
@@ -46,7 +46,9 @@
     step_dir = adamw_step(master, moment_one, moment_two, gradient)
     updated = master - learn_rate * step_dir
     weights = updated.astype(jnp.bfloat16)
-    gathered = lax.all_gather(weights, "grp", axis=1, tiled=True)
+    gathered = jnp.concatenate(
+        lax.all_to_all(jnp.stack([weights] * lax.axis_size("grp")), "grp", 0, 0), axis=1
+    )
     shift = groups // 2
     backup = lax.ppermute(step_dir, "grp", [(s, (s + shift) % groups) for s in range(groups)])
     pairs = tok_count * top_count

time: 427 us -> 442 us (1.035)
  the two profiles are of different devices: /device:TPU:21 before, /device:TPU:34 now
where the time goes in v2:
time: 442 us; the launch traced here: 441 us
  waiting for transfers between devices  357 us (81%)
  starting transfers between devices  44.4 us (10%)
  matrix products  17.7 us (4%)
  local copies, waits for them, and re-layouts  15.6 us (4%)
  other arithmetic  5.13 us (1%)
    all_to_all x1, waiting for transfers between devices, body(): lax.all_to_all(tiles, 'ep', split_axis=0, concat_axis=0, tiled=True)  150 us
    all_to_all x1, waiting for transfers between devices, body(): lax.all_to_all(jnp.stack([weights] * lax.axis_size('grp')), 'grp', 0, 0)  132 us
    all_to_all x1, waiting for transfers between devices, body(): lax.all_to_all(outgoing, 'ep', split_axis=0, concat_axis=1, tiled=True)  58.3 us
    all_to_all x1, starting transfers between devices, body(): lax.all_to_all(tiles, 'ep', split_axis=0, concat_axis=0, tiled=True)  18 us
    ppermute x1, waiting for transfers between devices, body(): lax.ppermute(step_dir, 'grp', [(s, (s + shift) % groups) for s in range(g...  17.4 us
    all_to_all x1, starting transfers between devices, body(): lax.all_to_all(outgoing, 'ep', split_axis=0, concat_axis=1, tiled=True)  15.9 us
  transfers between devices with their start and end apart: 4, of which 4 were waited for; matrix products, arithmetic and copies ran while one was open for 2% of the time, Pallas kernels for 0%

profile of v2, /device:TPU:34, one launch (start us, length us, event | category | flops | bytes accessed | tf_op | source)
XLA Modules:
  0.0 441.2 jit_solution(8775398326669913367)
XLA Ops:
  0.6 0.0 copy-start
  0.6 0.9 copy.32
  1.6 0.1 eq.31
  1.6 0.5 convert_reduce_fusion
  2.2 0.0 copy-done
  2.2 0.0 copy-start.2
  2.2 0.0 copy-start.3
  2.2 0.0 copy-start.4
  2.2 4.0 fusion.2
  6.3 15.9 %all-to-all-start = ((bf16[64,24,768]{2,1,0:T(8,128)(2,1)}), bf16[64,24,768]{2,1,0:T(8,128)(2,1)}, u32[]{:S(2)}, u32[]{:S(2)}) async-start(bf16[64,24,768]{2,1,0:T(8,128)(2,1)} %bitcast.22), calls=%async_computation | async-start | bytes 4718592 | tf_op jit(solution)/shard_map/all_to_all | solution.py:62
  22.1 0.0 copy-done.2
  22.2 0.0 copy-done.3
  22.2 0.0 copy-done.4
  22.2 2.6 subtract_convert_fusion.1
  24.7 58.3 %all-to-all-done = bf16[64,24,768]{2,1,0:T(8,128)(2,1)} async-done(((bf16[64,24,768]{2,1,0:T(8,128)(2,1)}), bf16[64,24,768]{2,1,0:T(8,128)(2,1)}, u32[]{:S(2)}, u32[]{:S(2)}) %all-to-all-start) | async-done | bytes 2359328 | tf_op jit(solution)/shard_map/all_to_all | solution.py:62
  83.0 3.4 stack.2
  86.5 7.2 %all-to-all-start.1 = ((bf16[16,2,48,2048]{3,2,1,0:T(8,128)(2,1)}), bf16[16,2,48,2048]{3,2,1,0:T(8,128)(2,1)}, u32[]{:S(2)}, u32[]{:S(2)}) async-start(bf16[16,2,48,2048]{3,2,1,0:T(8,128)(2,1)} %stack.2), calls=%async_computation.1 | async-start | bytes 12582912 | tf_op jit(solution)/shard_map/all_to_all | solution.py:50
  93.7 3.2 copy.36
  96.9 132.0 %all-to-all-done.1 = bf16[16,2,48,2048]{3,2,1,0:T(8,128)(2,1)} async-done(((bf16[16,2,48,2048]{3,2,1,0:T(8,128)(2,1)}), bf16[16,2,48,2048]{3,2,1,0:T(8,128)(2,1)}, u32[]{:S(2)}, u32[]{:S(2)}) %all-to-all-start.1) | async-done | bytes 6291488 | tf_op jit(solution)/shard_map/all_to_all | solution.py:50
  228.9 0.0 copy-start.1
  228.9 3.5 copy.37
  232.4 0.0 copy-done.1
  232.4 5.3 %multiply_convert_fusion = bf16[2,768,2048]{2,1,0:T(8,128)(2,1)S(1)} fusion(bf16[2,768,768]{2,1,0:T(8,128)(2,1)S(1)} %bitcast.23, bf16[2,768,2048]{2,1,0:T(8,128)(2,1)S(1)} %bitcast.20), kind=kOutput, calls=%fused_computation | convolution fusion | flops 4838129664 | bytes 14942208 | tf_op jit(solution)/shard_map/erh,ehd->erd/dot_general | solution.py:63
  237.6 3.2 copy.40
  240.9 0.0 copy-start.5
  240.9 0.0 copy-start.6
  240.9 18.0 %all-to-all-start.2 = ((bf16[32,2,24,2048]{3,2,1,0:T(8,128)(2,1)}), bf16[32,2,24,2048]{3,2,1,0:T(8,128)(2,1)}, u32[]{:S(2)}, u32[]{:S(2)}) async-start(bf16[32,2,24,2048]{3,2,1,0:T(8,128)(2,1)} %bitcast.19), calls=%async_computation.2 | async-start | bytes 12582912 | tf_op jit(solution)/shard_map/all_to_all | solution.py:66
  258.8 3.4 collective-permute-start
  262.2 0.1 reduce_sum.21
  262.4 0.0 copy-done.5
  262.4 0.1 copy.34
  262.5 0.0 copy-done.6
  262.5 0.1 copy.35
  262.6 2.0 select_reduce_fusion
  264.7 17.4 %collective-permute-done = f32[2,48,2048]{2,1,0:T(8,128)S(1)} collective-permute-done((f32[2,48,2048]{2,1,0:T(8,128)}, f32[2,48,2048]{2,1,0:T(8,128)S(1)}, u32[]{:S(2)}, u32[]{:S(2)}) %collective-permute-start) | collective-permute-done | bytes 786464 | tf_op jit(solution)/shard_map/ppermute | solution.py:53
  282.0 149.8 %all-to-all-done.2 = bf16[32,2,24,2048]{3,2,1,0:T(8,128)(2,1)} async-done(((bf16[32,2,24,2048]{3,2,1,0:T(8,128)(2,1)}), bf16[32,2,24,2048]{3,2,1,0:T(8,128)(2,1)}, u32[]{:S(2)}, u32[]{:S(2)}) %all-to-all-start.2) | async-done | bytes 6291488 | tf_op jit(solution)/shard_map/all_to_all | solution.py:66
  431.9 3.8 fusion.15
  435.7 4.6 %fusion.4 = bf16[128,2048]{1,0:T(8,128)(2,1)} fusion(f32[128,2048]{1,0:T(8,128)S(1)} %fusion.15, bf16[1536,2048]{1,0:T(8,128)(2,1)} %bitcast.9, f32[128,1536]{1,0:T(8,128)S(1)} %select_reduce_fusion), kind=kOutput, calls=%fused_computation.12 | convolution fusion | flops 806617088 | bytes 8650752 | tf_op jit(solution)/shard_map/dot_general | solution.py:76
  440.3 0.9 copy.42
  (4 shorter events, 0.1 us)
Async XLA Ops:
  0.6 1.6 copy-start
  2.2 20.0 %copy-start.2 = (f32[2,48,2048]{2,1,0:T(8,128)S(1)}, f32[2,48,2048]{2,1,0:T(8,128)}, u32[]{:S(2)}) copy-start(f32[2,48,2048]{2,1,0:T(8,128)} %param.10) | copy-start | bytes 2359300
  2.2 20.0 %copy-start.3 = (bf16[2,48,2048]{2,1,0:T(8,128)(2,1)S(1)}, bf16[2,48,2048]{2,1,0:T(8,128)(2,1)}, u32[]{:S(2)}) copy-start(bf16[2,48,2048]{2,1,0:T(8,128)(2,1)} %param.12) | copy-start | bytes 1179652
  2.2 20.0 %copy-start.4 = (bf16[2,48,2048]{2,1,0:T(8,128)(2,1)S(1)}, bf16[2,48,2048]{2,1,0:T(8,128)(2,1)}, u32[]{:S(2)}) copy-start(bf16[2,48,2048]{2,1,0:T(8,128)(2,1)} %param.13) | copy-start | bytes 1179652
  6.3 76.8 %all-to-all-start = ((bf16[64,24,768]{2,1,0:T(8,128)(2,1)}), bf16[64,24,768]{2,1,0:T(8,128)(2,1)}, u32[]{:S(2)}, u32[]{:S(2)}) async-start(bf16[64,24,768]{2,1,0:T(8,128)(2,1)} %bitcast.22), calls=%async_computation | async-start | bytes 4718592 | tf_op jit(solution)/shard_map/all_to_all | solution.py:62
  86.5 142.4 %all-to-all-start.1 = ((bf16[16,2,48,2048]{3,2,1,0:T(8,128)(2,1)}), bf16[16,2,48,2048]{3,2,1,0:T(8,128)(2,1)}, u32[]{:S(2)}, u32[]{:S(2)}) async-start(bf16[16,2,48,2048]{3,2,1,0:T(8,128)(2,1)} %stack.2), calls=%async_computation.1 | async-start | bytes 12582912 | tf_op jit(solution)/shard_map/all_to_all | solution.py:50
  228.9 3.5 copy-start.1
  240.9 21.5 %copy-start.5 = (s32[128,8]{0,1:T(8,128)S(1)}, s32[128,8]{0,1:T(8,128)}, u32[]{:S(2)}) copy-start(s32[128,8]{0,1:T(8,128)} %param.8) | copy-start | bytes 12292
  240.9 21.7 %copy-start.6 = (s32[128,8]{0,1:T(8,128)S(1)}, s32[128,8]{0,1:T(8,128)}, u32[]{:S(2)}) copy-start(s32[128,8]{0,1:T(8,128)} %param.9) | copy-start | bytes 12292
  240.9 191.0 %all-to-all-start.2 = ((bf16[32,2,24,2048]{3,2,1,0:T(8,128)(2,1)}), bf16[32,2,24,2048]{3,2,1,0:T(8,128)(2,1)}, u32[]{:S(2)}, u32[]{:S(2)}) async-start(bf16[32,2,24,2048]{3,2,1,0:T(8,128)(2,1)} %bitcast.19), calls=%async_computation.2 | async-start | bytes 12582912 | tf_op jit(solution)/shard_map/all_to_all | solution.py:66
  258.8 23.2 %collective-permute-start = (f32[2,48,2048]{2,1,0:T(8,128)}, f32[2,48,2048]{2,1,0:T(8,128)S(1)}, u32[]{:S(2)}, u32[]{:S(2)}) collective-permute-start(f32[2,48,2048]{2,1,0:T(8,128)} %get-tuple-element.3), channel_id=1, source_target_pairs={{0,256},{32,288},{64,320},{96,352},{128,384},{160,416},{192,448},{... | collective-permute-start | bytes 2359304 | tf_op jit(solution)/shard_map/ppermute | solution.py:53
